TPU v7x, 256 devices: a whole 4x4x8 slice. The times are simulated.
256 devices in a mesh: link: 64 (over x, z, core), col: 4 (over y).
Axes of the slice: x: 4, y: 4, z: 8, core: 2. Of those that a mesh axis runs over, the one named last changes fastest.
Arguments:
- values: bfloat16 [1024, 16, 128], P('link'), may hold values from -6 to 6
- tiles: int32 [1024, 16], P('link'), may hold values from 0 to 127, all different within a row
- barrier: float32 [1024], P('link'), may hold values from 0.5 to 2
- slack: float32 [16384], replicated, may hold values from 0.5 to 2
- order: int32 [128], replicated, may hold values from 0 to 127, each once
Outputs:
- factored: float32 [16384, 16384], P('link', 'col')
Inputs may be any that keep to these rules, and one draw needn't show every extreme that they name: `tiles`: each commodity's 16 tile numbers are distinct, and every tile is named by some commodity. `order`: each tile number appears once.
All inputs are finite; a program needn't handle non-finite values.
Results may differ from a plain program's by a relative error of at most 0.0038.
Values may be sent and summed in bfloat16 or wider, within the bound.
No kernel may reach another device: no remote copies, remote signals or barrier semaphores. Data moves between devices by JAX's collectives and lax.ppermute only.
A program may use at most 64 MiB of HBM per device.

v0:
```python
import jax
import jax.numpy as jnp
from jax import lax
from jax.sharding import PartitionSpec as P

PANEL = 128


def spread(value, axis, source):
    kept = jnp.where(lax.axis_index(axis) == source, value, 0).astype(value.dtype)
    return lax.psum(kept, axis)


def densify(tile_vals, tile_ids, targets):
    onehot = (tile_ids[:, :, None] == targets[None, None, :]).astype(jnp.bfloat16)
    dense_out = jnp.einsum("kjp,kju->kpu", onehot, tile_vals, preferred_element_type=jnp.float32)
    dense_out = dense_out.astype(jnp.bfloat16)
    return dense_out.reshape(tile_vals.shape[0], targets.shape[0] * tile_vals.shape[2])


def contract_rows(left_side, right_side):
    return lax.dot_general(
        left_side, right_side, (((0,), (0,)), ((), ())), preferred_element_type=jnp.float32
    )


def local(values, tiles, barrier, slack, order):
    link_devs = lax.axis_size("link")
    col_devs = lax.axis_size("col")
    link_idx = lax.axis_index("link")
    col_idx = lax.axis_index("col")
    link_count = slack.shape[0]
    rows_dev = link_count // link_devs
    cols_dev = link_count // col_devs
    tile_len = values.shape[2]
    ntiles = order.shape[0]
    factor = link_count / (values.shape[0] * link_devs * values.shape[1] * tile_len)
    scaled = (jnp.sqrt(barrier * factor)[:, None, None] * values.astype(jnp.float32)).astype(
        jnp.bfloat16
    )
    own_dense = densify(scaled, tiles, order)
    link_rows = lax.all_to_all(own_dense, "link", split_axis=1, concat_axis=0, tiled=True)
    col_slab = lax.dynamic_slice_in_dim(own_dense, col_idx * cols_dev, cols_dev, 1)
    normal = contract_rows(link_rows, lax.all_gather(col_slab, "link", axis=0, tiled=True))
    rows_g = link_idx * rows_dev + jnp.arange(rows_dev)
    cols_g = col_idx * cols_dev + jnp.arange(cols_dev)
    perm_hot = (order[:, None] == jnp.arange(ntiles)[None, :]).astype(jnp.float32)
    slack_ord = jnp.dot(
        perm_hot, slack.reshape(ntiles, tile_len), precision=lax.Precision.HIGHEST
    ).reshape(link_count)
    slack_rows = lax.dynamic_slice_in_dim(slack_ord, link_idx * rows_dev, rows_dev)
    matrix = normal + jnp.where(
        rows_g[:, None] == cols_g[None, :], slack_rows[:, None], jnp.float32(0.0)
    )
    panels = []
    for panel_no in range(2):
        first_col = panel_no * PANEL
        diag_block = matrix[first_col : first_col + PANEL, first_col : first_col + PANEL]
        factor_local = jnp.linalg.cholesky(diag_block)
        lower_fac = spread(factor_local, "link", 0)
        solved = jax.scipy.linalg.solve_triangular(
            lower_fac, matrix[:, first_col : first_col + PANEL].T, lower=True
        ).T
        picker = ((rows_g - first_col)[:, None] == jnp.arange(PANEL)[None, :]).astype(jnp.float32)
        diag_rows = jnp.dot(picker, lower_fac, precision=lax.Precision.HIGHEST)
        column = jnp.where(
            rows_g[:, None] < first_col,
            jnp.float32(0.0),
            jnp.where(rows_g[:, None] < first_col + PANEL, diag_rows, solved),
        )
        across = spread(column.astype(jnp.bfloat16), "col", 0)
        everyone = lax.all_gather(across, "link", axis=0, tiled=True)
        col_part = lax.dynamic_slice_in_dim(everyone, col_idx * cols_dev, cols_dev, 0)
        matrix = matrix - lax.dot_general(
            across, col_part, (((1,), (1,)), ((), ())), preferred_element_type=jnp.float32
        )
        panels.append(column)
    panel_block = jnp.concatenate(panels, 1)
    padded = jnp.pad(panel_block, ((0, 0), (0, cols_dev - 2 * PANEL)))
    return jnp.where(
        cols_g[None, :] < 2 * PANEL,
        padded,
        jnp.where(rows_g[:, None] < 2 * PANEL, jnp.float32(0.0), matrix),
    )


def solution(mesh):
    in_specs = (P("link", None, None), P("link", None), P("link"), P(), P())
    out_specs = P("link", "col")
    return jax.shard_map(local, mesh=mesh, in_specs=in_specs, out_specs=out_specs, check_vma=False)
```

profile of v0, /device:TPU:1, one launch (start us, length us, event | category | flops | bytes accessed | tf_op | source)
XLA Modules:
  0.0 768.8 jit_solution(11925922518593524493)
XLA Ops:
  6.5 0.7 multiply_sqrt_fusion
  7.2 1.4 convolution_convert_fusion
  8.6 0.3 copy.24
  9.0 0.7 constant_dynamic-slice_fusion
  9.7 0.0 all-gather.4.cloned.1.call-update
  9.7 0.2 all_to_all.14
  9.9 1.1 copy.12
  10.9 13.0 %all-to-all-start = ((bf16[16,64,256]{2,0,1:T(8,128)(2,1)}), bf16[16,64,256]{2,0,1:T(8,128)(2,1)S(1)}, u32[]{:S(2)}, u32[]{:S(2)}) async-start(bf16[16,64,256]{2,0,1:T(8,128)(2,1)} %copy.12), calls=%async_computation | async-start | bytes 1048576 | tf_op jit(solution)/shard_map/all_to_all | solution.py:42
  23.9 0.0 all-reduce.6.cloned.1.call-start
  24.0 0.2 convolution_bitcast_fusion
  24.2 0.1 dynamic_slice.13
  24.3 19.3 %all-to-all-done = bf16[16,64,256]{2,0,1:T(8,128)(2,1)S(1)} async-done(((bf16[16,64,256]{2,0,1:T(8,128)(2,1)}), bf16[16,64,256]{2,0,1:T(8,128)(2,1)S(1)}, u32[]{:S(2)}, u32[]{:S(2)}) %all-to-all-start) | async-done | bytes 524320 | tf_op jit(solution)/shard_map/all_to_all | solution.py:42
  43.6 54.6 %all-gather.4.cloned.1.call-done = bf16[1024,4096]{1,0:T(8,128)(2,1)} async-done(((bf16[16,4096]{1,0:T(8,128)(2,1)}), bf16[1024,4096]{1,0:T(8,128)(2,1)}) %all-gather.4.cloned.1.call-update) | async-done | bytes 8388624 | tf_op jit(solution)/shard_map/all_gather | solution.py:44
  98.2 6.6 convolution_add_fusion
  104.8 2.0 copy-done.1
  106.8 0.1 copy.14
  106.9 0.9 fusion.14
  107.8 11.7 %cholesky.44 = f32[128,128]{1,0:T(8,128)S(1)} custom-call(f32[128,128]{1,0:T(8,128)S(1)} %fusion.14), custom_call_target="Cholesky" | custom-call | tf_op jit(solution)/shard_map/jit(cholesky)/cholesky | solution.py:59
  119.5 0.7 compare_reduce_fusion.1
  120.2 1.3 select_select_fusion.1
  121.5 0.0 all-reduce.8.cloned.1.call-start
  121.6 167.5 %all-reduce.6.cloned.1.call-done = f32[128,128]{1,0:T(8,128)} async-done(((f32[128,128]{1,0:T(8,128)}), f32[128,128]{1,0:T(8,128)}) %all-reduce.6.cloned.1.call-update) | async-done | bytes 65552 | tf_op jit(solution)/shard_map/psum | solution.py:11
  289.1 0.8 select_bitcast_fusion.1
  289.9 9.8 %custom-call.6 = f32[1,128,128]{1,2,0:T(8,128)S(1)} custom-call(f32[1,128,128]{2,1,0:T(8,128)S(1)} %select_bitcast_fusion.1), custom_call_target="InvertDiagBlocksLowerTriangular" | custom-call | tf_op jit(solution)/shard_map/jit(_solve_triangular)/triangular_solve | solution.py:61
  299.7 1.1 fusion.8
  300.9 1.9 convert_select_fusion.1
  302.8 0.0 all-gather.6.cloned.1.call-start
  302.8 41.2 %all-reduce.8.cloned.1.call-done = bf16[256,128]{0,1:T(8,128)(2,1)} async-done(((bf16[256,128]{0,1:T(8,128)(2,1)}), bf16[256,128]{0,1:T(8,128)(2,1)}) %all-reduce.8.cloned.1.call-update) | async-done | bytes 65552 | tf_op jit(solution)/shard_map/psum | solution.py:11
  344.0 0.2 all-reduce.10.cloned.1.call-start
  344.3 81.0 %all-gather.6.cloned.1.call-done = bf16[16384,128]{0,1:T(8,128)(2,1)} async-done(((bf16[256,128]{0,1:T(8,128)(2,1)}), bf16[16384,128]{0,1:T(8,128)(2,1)}) %all-gather.6.cloned.1.call-update) | async-done | bytes 4194320 | tf_op jit(solution)/shard_map/all_gather | solution.py:72
  425.2 3.3 convolution_subtract_fusion.1
  428.6 2.0 copy-done.2
  430.6 0.1 copy.16
  430.7 0.9 fusion.12
  431.5 11.7 %cholesky.55 = f32[128,128]{1,0:T(8,128)S(1)} custom-call(f32[128,128]{1,0:T(8,128)S(1)} %fusion.12), custom_call_target="Cholesky" | custom-call | tf_op jit(solution)/shard_map/jit(cholesky)/cholesky | solution.py:59
  443.3 0.7 compare_reduce_fusion
  443.9 1.3 select_select_fusion
  445.2 0.0 all-reduce.12.cloned.1.call-start
  445.3 170.2 %all-reduce.10.cloned.1.call-done = f32[128,128]{1,0:T(8,128)} async-done(((f32[128,128]{1,0:T(8,128)}), f32[128,128]{1,0:T(8,128)}) %all-reduce.10.cloned.1.call-update) | async-done | bytes 65552 | tf_op jit(solution)/shard_map/psum | solution.py:11
  615.4 0.8 select_bitcast_fusion
  616.3 9.8 %custom-call.7 = f32[1,128,128]{1,2,0:T(8,128)S(1)} custom-call(f32[1,128,128]{2,1,0:T(8,128)S(1)} %select_bitcast_fusion), custom_call_target="InvertDiagBlocksLowerTriangular" | custom-call | tf_op jit(solution)/shard_map/jit(_solve_triangular)/triangular_solve | solution.py:61
  626.1 1.1 fusion.9
  627.3 1.9 convert_select_fusion
  629.1 0.0 all-gather.8.cloned.1.call-start
  629.2 41.2 %all-reduce.12.cloned.1.call-done = bf16[256,128]{0,1:T(8,128)(2,1)} async-done(((bf16[256,128]{0,1:T(8,128)(2,1)}), bf16[256,128]{0,1:T(8,128)(2,1)}) %all-reduce.12.cloned.1.call-update) | async-done | bytes 65552 | tf_op jit(solution)/shard_map/psum | solution.py:11
  670.4 81.4 %all-gather.8.cloned.1.call-done = bf16[16384,128]{0,1:T(8,128)(2,1)} async-done(((bf16[256,128]{0,1:T(8,128)(2,1)}), bf16[16384,128]{0,1:T(8,128)(2,1)}) %all-gather.8.cloned.1.call-update) | async-done | bytes 4194320 | tf_op jit(solution)/shard_map/all_gather | solution.py:72
  751.8 4.6 fusion.1
  756.3 5.6 copy.18
  (23 shorter events, 0.2 us)
Async XLA Ops:
  6.5 17.5 %copy-start = (f32[16384]{0:T(1024)S(1)}, f32[16384]{0:T(1024)}, u32[]{:S(2)}) copy-start(f32[16384]{0:T(1024)} %param.11) | copy-start | bytes 196612
  6.5 17.5 %copy-start.3 = (s32[128]{0:T(128)S(1)}, s32[128]{0:T(128)}, u32[]{:S(2)}) copy-start(s32[128]{0:T(128)} %param.12) | copy-start | bytes 1540
  6.5 91.6 %all-gather.4.cloned.1.call-start = ((), (), s32[]{:S(2)}) async-start(), calls=%async_computation.1 | async-start | bytes 8519680 | tf_op jit(solution)/shard_map/all_gather | solution.py:44
  10.9 32.7 %all-to-all-start = ((bf16[16,64,256]{2,0,1:T(8,128)(2,1)}), bf16[16,64,256]{2,0,1:T(8,128)(2,1)S(1)}, u32[]{:S(2)}, u32[]{:S(2)}) async-start(bf16[16,64,256]{2,0,1:T(8,128)(2,1)} %copy.12), calls=%async_computation | async-start | bytes 1048576 | tf_op jit(solution)/shard_map/all_to_all | solution.py:42
  23.9 265.1 %all-reduce.6.cloned.1.call-start = ((), (), s32[]{:S(2)}) async-start(), calls=%async_computation.2 | async-start | bytes 131072 | tf_op jit(solution)/shard_map/psum | solution.py:11
  104.8 2.0 copy-start.1
  121.5 222.5 %all-reduce.8.cloned.1.call-start = ((), (), s32[]{:S(2)}) async-start(), calls=%async_computation.3 | async-start | bytes 131072 | tf_op jit(solution)/shard_map/psum | solution.py:11
  302.8 122.5 %all-gather.6.cloned.1.call-start = ((), (), s32[]{:S(2)}) async-start(), calls=%async_computation.4 | async-start | bytes 4259840 | tf_op jit(solution)/shard_map/all_gather | solution.py:72
  344.0 271.4 %all-reduce.10.cloned.1.call-start = ((), (), s32[]{:S(2)}) async-start(), calls=%async_computation.5 | async-start | bytes 131072 | tf_op jit(solution)/shard_map/psum | solution.py:11
  428.5 2.0 copy-start.2
  445.2 225.1 %all-reduce.12.cloned.1.call-start = ((), (), s32[]{:S(2)}) async-start(), calls=%async_computation.6 | async-start | bytes 131072 | tf_op jit(solution)/shard_map/psum | solution.py:11
  629.1 122.6 %all-gather.8.cloned.1.call-start = ((), (), s32[]{:S(2)}) async-start(), calls=%async_computation.7 | async-start | bytes 4259840 | tf_op jit(solution)/shard_map/all_gather | solution.py:72
Sparse Core Ops, SparseCore 0:
  10.1 88.0 all-gather.3
  121.6 167.4 all-reduce.5
  302.9 41.0 all-reduce.7
  346.4 78.8 all-gather.5
  445.3 170.0 all-reduce.9
  629.3 41.0 all-reduce.11
  672.9 78.8 all-gather.7
where the time goes:
time: 769 us
  waiting for transfers between devices  656 us (85%)
  other arithmetic  51.1 us (7%)
  matrix products  22.1 us (3%)
  between operations  13.7 us (2%)
  starting transfers between devices  13.4 us (2%)
  local copies, waits for them, and re-layouts  12.1 us (2%)
    psum x4, waiting for transfers between devices, spread(): return lax.psum(kept, axis)  420 us
    all_gather x2, waiting for transfers between devices, local(): everyone = lax.all_gather(across, 'link', axis=0, tiled=True)  162 us
    all_gather x1, waiting for transfers between devices, local(): lax.all_gather(col_slab, 'link', axis=0, tiled=True)  54.6 us
    another operation x6, other arithmetic, local(): factor_local = jnp.linalg.cholesky(diag_block)  24.8 us
    another operation x4, other arithmetic, local(): jax.scipy.linalg.solve_triangular(lower_fac, matrix[:, first_col:first_co...  21.3 us
    all_to_all x1, waiting for transfers between devices, local(): lax.all_to_all(own_dense, 'link', split_axis=1, concat_axis=0, tiled=True)  19.3 us
  transfers between devices with their start and end apart: 8, of which 8 were waited for; matrix products, arithmetic and copies ran while one was open for 0% of the time, Pallas kernels for 0%

commit v1 on v0

--- a/solution.py
+++ b/solution.py
@@ -69,7 +69,9 @@
             jnp.where(rows_g[:, None] < first_col + PANEL, diag_rows, solved),
         )
         across = spread(column.astype(jnp.bfloat16), "col", 0)
-        everyone = lax.all_gather(across, "link", axis=0, tiled=True)
+        everyone = jnp.concatenate(
+            lax.all_to_all(jnp.stack([across] * lax.axis_size("link")), "link", 0, 0), axis=0
+        )
         col_part = lax.dynamic_slice_in_dim(everyone, col_idx * cols_dev, cols_dev, 0)
         matrix = matrix - lax.dot_general(
             across, col_part, (((1,), (1,)), ((), ())), preferred_element_type=jnp.float32

time: 769 us -> 829 us (1.078)
  waiting for transfers between devices: 656 us -> 682 us
  starting transfers between devices: 13.4 us -> 39.1 us
    all_to_all x0 -> x2, waiting for transfers between devices: none -> 192 us  [local(): lax.all_to_all(jnp.stack([across] * lax.axis_size('link')), 'link', 0, 0)]
    all_gather x2 -> x0, waiting for transfers between devices: 162 us -> none  [local(): everyone = lax.all_gather(across, 'link', axis=0, tiled=True)]
    all_to_all x0 -> x2, starting transfers between devices: none -> 26 us  [local(): lax.all_to_all(jnp.stack([across] * lax.axis_size('link')), 'link', 0, 0)]
where the time goes in v1:
time: 829 us; the launch traced here: 828 us
  waiting for transfers between devices  682 us (82%)
  other arithmetic  51.1 us (6%)
  starting transfers between devices  39.1 us (5%)
  matrix products  21.9 us (3%)
  local copies, waits for them, and re-layouts  20 us (2%)
  between operations  13.4 us (2%)
    psum x4, waiting for transfers between devices, spread(): return lax.psum(kept, axis)  416 us
    all_to_all x2, waiting for transfers between devices, local(): lax.all_to_all(jnp.stack([across] * lax.axis_size('link')), 'link', 0, 0)  192 us
    all_gather x1, waiting for transfers between devices, local(): lax.all_gather(col_slab, 'link', axis=0, tiled=True)  54.6 us
    all_to_all x2, starting transfers between devices, local(): lax.all_to_all(jnp.stack([across] * lax.axis_size('link')), 'link', 0, 0)  26 us
    another operation x6, other arithmetic, local(): factor_local = jnp.linalg.cholesky(diag_block)  24.8 us
    another operation x4, other arithmetic, local(): jax.scipy.linalg.solve_triangular(lower_fac, matrix[:, first_col:first_co...  21.3 us
    all_to_all x1, waiting for transfers between devices, local(): lax.all_to_all(own_dense, 'link', split_axis=1, concat_axis=0, tiled=True)  19.3 us
  transfers between devices with their start and end apart: 8, of which 8 were waited for; matrix products, arithmetic and copies ran while one was open for 0% of the time, Pallas kernels for 0%

profile of v1, /device:TPU:1, one launch (start us, length us, event | category | flops | bytes accessed | tf_op | source)
XLA Modules:
  0.0 827.5 jit_solution(10599890348467425141)
XLA Ops:
  6.5 0.7 multiply_sqrt_fusion
  7.2 1.4 convolution_convert_fusion
  8.6 0.3 copy.28
  9.0 0.7 constant_dynamic-slice_fusion
  9.7 0.2 all_to_all.20
  9.9 1.1 copy.14
  10.9 13.0 %all-to-all-start = ((bf16[16,64,256]{2,0,1:T(8,128)(2,1)}), bf16[16,64,256]{2,0,1:T(8,128)(2,1)S(1)}, u32[]{:S(2)}, u32[]{:S(2)}) async-start(bf16[16,64,256]{2,0,1:T(8,128)(2,1)} %copy.14), calls=%async_computation | async-start | bytes 1048576 | tf_op jit(solution)/shard_map/all_to_all | solution.py:42
  23.9 0.0 all-reduce.6.cloned.1.call-start
  24.0 0.2 convolution_bitcast_fusion
  24.2 0.1 dynamic_slice.13
  24.3 19.3 %all-to-all-done = bf16[16,64,256]{2,0,1:T(8,128)(2,1)S(1)} async-done(((bf16[16,64,256]{2,0,1:T(8,128)(2,1)}), bf16[16,64,256]{2,0,1:T(8,128)(2,1)S(1)}, u32[]{:S(2)}, u32[]{:S(2)}) %all-to-all-start) | async-done | bytes 524320 | tf_op jit(solution)/shard_map/all_to_all | solution.py:42
  43.6 54.6 %all-gather.2.cloned.1.call-done = bf16[1024,4096]{1,0:T(8,128)(2,1)} async-done(((bf16[16,4096]{1,0:T(8,128)(2,1)}), bf16[1024,4096]{1,0:T(8,128)(2,1)}) %all-gather.2.cloned.1.call-update) | async-done | bytes 8388624 | tf_op jit(solution)/shard_map/all_gather | solution.py:44
  98.2 6.6 convolution_add_fusion
  104.8 2.0 copy-done.1
  106.8 0.1 copy.16
  106.9 0.9 fusion.14
  107.8 11.7 %cholesky.44 = f32[128,128]{1,0:T(8,128)S(1)} custom-call(f32[128,128]{1,0:T(8,128)S(1)} %fusion.14), custom_call_target="Cholesky" | custom-call | tf_op jit(solution)/shard_map/jit(cholesky)/cholesky | solution.py:59
  119.5 0.7 compare_reduce_fusion.1
  120.2 1.3 select_select_fusion.1
  121.6 167.5 %all-reduce.6.cloned.1.call-done = f32[128,128]{1,0:T(8,128)} async-done(((f32[128,128]{1,0:T(8,128)}), f32[128,128]{1,0:T(8,128)}) %all-reduce.6.cloned.1.call-update) | async-done | bytes 65552 | tf_op jit(solution)/shard_map/psum | solution.py:11
  289.1 0.8 select_bitcast_fusion.1
  289.9 9.8 %custom-call.6 = f32[1,128,128]{1,2,0:T(8,128)S(1)} custom-call(f32[1,128,128]{2,1,0:T(8,128)S(1)} %select_bitcast_fusion.1), custom_call_target="InvertDiagBlocksLowerTriangular" | custom-call | tf_op jit(solution)/shard_map/jit(_solve_triangular)/triangular_solve | solution.py:61
  299.7 1.1 fusion.8
  300.9 1.9 convert_select_fusion.1
  302.8 41.2 %all-reduce.8.cloned.1.call-done = bf16[256,128]{0,1:T(8,128)(2,1)} async-done(((bf16[256,128]{0,1:T(8,128)(2,1)}), bf16[256,128]{0,1:T(8,128)(2,1)}) %all-reduce.8.cloned.1.call-update) | async-done | bytes 65552 | tf_op jit(solution)/shard_map/psum | solution.py:11
  344.0 0.9 copy.17
  344.9 3.0 stack.4
  347.9 13.0 %all-to-all-start.1 = ((bf16[64,256,128]{2,1,0:T(8,128)(2,1)}), bf16[64,256,128]{2,1,0:T(8,128)(2,1)}, u32[]{:S(2)}, u32[]{:S(2)}) async-start(bf16[64,256,128]{2,1,0:T(8,128)(2,1)} %stack.4), calls=%async_computation.1 | async-start | bytes 8388608 | tf_op jit(solution)/shard_map/all_to_all | solution.py:73
  361.0 95.8 %all-to-all-done.1 = bf16[64,256,128]{2,1,0:T(8,128)(2,1)} async-done(((bf16[64,256,128]{2,1,0:T(8,128)(2,1)}), bf16[64,256,128]{2,1,0:T(8,128)(2,1)}, u32[]{:S(2)}, u32[]{:S(2)}) %all-to-all-start.1) | async-done | bytes 4194336 | tf_op jit(solution)/shard_map/all_to_all | solution.py:73
  456.8 3.2 convolution_subtract_fusion.1
  460.0 2.0 copy-done.2
  462.0 0.1 copy.19
  462.1 0.9 fusion.12
  463.0 11.7 %cholesky.55 = f32[128,128]{1,0:T(8,128)S(1)} custom-call(f32[128,128]{1,0:T(8,128)S(1)} %fusion.12), custom_call_target="Cholesky" | custom-call | tf_op jit(solution)/shard_map/jit(cholesky)/cholesky | solution.py:59
  474.7 0.7 compare_reduce_fusion
  475.4 1.3 select_select_fusion
  476.7 166.5 %all-reduce.10.cloned.1.call-done = f32[128,128]{1,0:T(8,128)} async-done(((f32[128,128]{1,0:T(8,128)}), f32[128,128]{1,0:T(8,128)}) %all-reduce.10.cloned.1.call-update) | async-done | bytes 65552 | tf_op jit(solution)/shard_map/psum | solution.py:11
  643.2 0.8 select_bitcast_fusion
  644.1 9.8 %custom-call.7 = f32[1,128,128]{1,2,0:T(8,128)S(1)} custom-call(f32[1,128,128]{2,1,0:T(8,128)S(1)} %select_bitcast_fusion), custom_call_target="InvertDiagBlocksLowerTriangular" | custom-call | tf_op jit(solution)/shard_map/jit(_solve_triangular)/triangular_solve | solution.py:61
  653.9 1.1 fusion.9
  655.0 1.9 convert_select_fusion
  656.9 41.2 %all-reduce.12.cloned.1.call-done = bf16[256,128]{0,1:T(8,128)(2,1)} async-done(((bf16[256,128]{0,1:T(8,128)(2,1)}), bf16[256,128]{0,1:T(8,128)(2,1)}) %all-reduce.12.cloned.1.call-update) | async-done | bytes 65552 | tf_op jit(solution)/shard_map/psum | solution.py:11
  698.1 0.9 copy.20
  699.1 3.0 stack.5
  702.1 13.0 %all-to-all-start.2 = ((bf16[64,256,128]{2,1,0:T(8,128)(2,1)}), bf16[64,256,128]{2,1,0:T(8,128)(2,1)}, u32[]{:S(2)}, u32[]{:S(2)}) async-start(bf16[64,256,128]{2,1,0:T(8,128)(2,1)} %stack.5), calls=%async_computation.2 | async-start | bytes 8388608 | tf_op jit(solution)/shard_map/all_to_all | solution.py:73
  715.1 95.8 %all-to-all-done.2 = bf16[64,256,128]{2,1,0:T(8,128)(2,1)} async-done(((bf16[64,256,128]{2,1,0:T(8,128)(2,1)}), bf16[64,256,128]{2,1,0:T(8,128)(2,1)}, u32[]{:S(2)}, u32[]{:S(2)}) %all-to-all-start.2) | async-done | bytes 4194336 | tf_op jit(solution)/shard_map/all_to_all | solution.py:73
  810.9 4.4 fusion.1
  815.4 5.6 copy.22
  (29 shorter events, 0.4 us)
Async XLA Ops:
  6.5 17.5 %copy-start = (f32[16384]{0:T(1024)S(1)}, f32[16384]{0:T(1024)}, u32[]{:S(2)}) copy-start(f32[16384]{0:T(1024)} %param.11) | copy-start | bytes 196612
  6.5 17.5 %copy-start.5 = (s32[128]{0:T(128)S(1)}, s32[128]{0:T(128)}, u32[]{:S(2)}) copy-start(s32[128]{0:T(128)} %param.12) | copy-start | bytes 1540
  6.5 91.6 %all-gather.2.cloned.1.call-start = ((), (), s32[]{:S(2)}) async-start(), calls=%async_computation.3 | async-start | bytes 8519680 | tf_op jit(solution)/shard_map/all_gather | solution.py:44
  10.9 32.7 %all-to-all-start = ((bf16[16,64,256]{2,0,1:T(8,128)(2,1)}), bf16[16,64,256]{2,0,1:T(8,128)(2,1)S(1)}, u32[]{:S(2)}, u32[]{:S(2)}) async-start(bf16[16,64,256]{2,0,1:T(8,128)(2,1)} %copy.14), calls=%async_computation | async-start | bytes 1048576 | tf_op jit(solution)/shard_map/all_to_all | solution.py:42
  23.9 265.1 %all-reduce.6.cloned.1.call-start = ((), (), s32[]{:S(2)}) async-start(), calls=%async_computation.4 | async-start | bytes 131072 | tf_op jit(solution)/shard_map/psum | solution.py:11
  104.8 2.0 copy-start.1
  121.5 222.5 %all-reduce.8.cloned.1.call-start = ((), (), s32[]{:S(2)}) async-start(), calls=%async_computation.5 | async-start | bytes 131072 | tf_op jit(solution)/shard_map/psum | solution.py:11
  347.9 108.8 %copy-start.3 = (bf16[256,128]{0,1:T(8,128)(2,1)S(1)}, bf16[256,128]{0,1:T(8,128)(2,1)}, u32[]{:S(2)}) copy-start(bf16[256,128]{0,1:T(8,128)(2,1)} %all-reduce.8.cloned.1.call-done) | copy-start | bytes 196612
  347.9 108.8 %all-to-all-start.1 = ((bf16[64,256,128]{2,1,0:T(8,128)(2,1)}), bf16[64,256,128]{2,1,0:T(8,128)(2,1)}, u32[]{:S(2)}, u32[]{:S(2)}) async-start(bf16[64,256,128]{2,1,0:T(8,128)(2,1)} %stack.4), calls=%async_computation.1 | async-start | bytes 8388608 | tf_op jit(solution)/shard_map/all_to_all | solution.py:73
  360.9 282.3 %all-reduce.10.cloned.1.call-start = ((), (), s32[]{:S(2)}) async-start(), calls=%async_computation.6 | async-start | bytes 131072 | tf_op jit(solution)/shard_map/psum | solution.py:11
  460.0 2.0 copy-start.2
  476.7 221.5 %all-reduce.12.cloned.1.call-start = ((), (), s32[]{:S(2)}) async-start(), calls=%async_computation.7 | async-start | bytes 131072 | tf_op jit(solution)/shard_map/psum | solution.py:11
  702.1 108.8 %copy-start.4 = (bf16[256,128]{0,1:T(8,128)(2,1)S(1)}, bf16[256,128]{0,1:T(8,128)(2,1)}, u32[]{:S(2)}) copy-start(bf16[256,128]{0,1:T(8,128)(2,1)} %all-reduce.12.cloned.1.call-done) | copy-start | bytes 196612
  702.1 108.8 %all-to-all-start.2 = ((bf16[64,256,128]{2,1,0:T(8,128)(2,1)}), bf16[64,256,128]{2,1,0:T(8,128)(2,1)}, u32[]{:S(2)}, u32[]{:S(2)}) async-start(bf16[64,256,128]{2,1,0:T(8,128)(2,1)} %stack.5), calls=%async_computation.2 | async-start | bytes 8388608 | tf_op jit(solution)/shard_map/all_to_all | solution.py:73
Sparse Core Ops, SparseCore 0:
  10.1 88.0 all-gather.1
  121.6 167.4 all-reduce.5
  302.9 41.0 all-reduce.7
  476.8 166.3 all-reduce.9
  657.0 41.0 all-reduce.11
